TPU v7x, 32 devices: a whole 2x2x4 slice. The times are simulated.
32 devices in a mesh: tile: 8 (over y, x, core), mem: 4 (over z).
Axes of the slice: x: 2, y: 2, z: 4, core: 2. Of those that a mesh axis runs over, the one named last changes fastest.
Arguments:
- control: bfloat16 [80, 1, 360, 720], P('mem', None, 'tile'), may hold values from -6 to 6
- perturb: bfloat16 [80, 1, 360, 720], P('mem', None, 'tile'), may hold values from -6 to 6
- lon_taps: bfloat16 [17], replicated, may hold values from 0.026367188 to 0.07910156
- lat_taps: bfloat16 [17], replicated, may hold values from 0.026367188 to 0.07910156
- innov: float32 [8, 8, 256], P('tile'), may hold values from -6 to 6
- inv_var: float32 [8, 8, 256], P('tile'), may hold values from 1 to 8
- cell_index: int32 [8, 8, 256], P('tile'), may hold values from 0 to 32399, as said below
- counts: int32 [8, 8], P('tile'), may hold values from 0 to 256, as said below
Outputs:
- gradient: float32 [80, 1, 360, 720], P('mem', None, 'tile')
Inputs may be any that keep to these rules, and one draw needn't show every extreme that they name: `cell_index`: an observation's cell within its owning tile, level * 45 * 720 + longitude within the tile * 720 + latitude; both ends are taken. `counts`: live slots per pair of tiles; some pair fills all 256 slots in every draw, and some owning tiles receive far more than others.
All inputs are finite; a program needn't handle non-finite values.
Results may differ from a plain program's by a relative error of at most 0.00066.
Values may be sent and summed in bfloat16 or wider, within the bound.
No kernel may reach another device: no remote copies, remote signals or barrier semaphores. Data moves between devices by JAX's collectives and lax.ppermute only.
A program may use at most 64 MiB of HBM per device.

v0:
```python
import math
import jax
import jax.numpy as jnp
from jax import lax
from jax.sharding import PartitionSpec as P


def extended_2(block, sides, width):
    for axis, dim in sides:
        count = lax.axis_size(axis)
        forward = [(i, i + 1) for i in range(count - 1)]
        forward.append((count - 1, 0))
        backward = [(target, source) for source, target in forward]
        low = lax.ppermute(
            lax.slice_in_dim(block, block.shape[dim] - width, None, axis=dim), axis, forward
        )
        high = lax.ppermute(lax.slice_in_dim(block, 0, width, axis=dim), axis, backward)
        block = jnp.concatenate([low, block, high], axis=dim)
    return block


def band_from(offsets, tap_weights):
    radius = tap_weights.shape[0] - 1
    taps = tap_weights.astype(jnp.float32)
    band = jnp.zeros(offsets.shape, jnp.float32)
    for offset in range(radius + 1):
        band = band + jnp.where(offsets == offset, taps[offset], 0.0)
    return band.astype(jnp.bfloat16)


def lon_band(tap_weights, lon_cells):
    radius = tap_weights.shape[0] - 1
    row_ids = lax.broadcasted_iota(jnp.int32, (lon_cells, lon_cells + 2 * radius), 0)
    col_ids = lax.broadcasted_iota(jnp.int32, (lon_cells, lon_cells + 2 * radius), 1)
    return band_from(jnp.abs(col_ids - row_ids - radius), tap_weights)


def lat_block_band(tap_weights, block_cells):
    radius = tap_weights.shape[0] - 1
    row_ids = lax.broadcasted_iota(jnp.int32, (block_cells + 2 * radius, block_cells), 0)
    col_ids = lax.broadcasted_iota(jnp.int32, (block_cells + 2 * radius, block_cells), 1)
    return band_from(jnp.abs(row_ids - radius - col_ids), tap_weights)


def localize(extended, band_lon, band_blocks, radius, block_cells):
    along = jnp.einsum(
        "ij,mljk->mlik", band_lon, extended, preferred_element_type=jnp.float32
    ).astype(jnp.bfloat16)
    members_here, levels, lon_cells, lat_cells = along.shape
    padded = jnp.pad(along, ((0, 0), (0, 0), (0, 0), (radius, radius)))
    block_count = lat_cells // block_cells
    windows = jnp.stack(
        [
            padded[:, :, :, block * block_cells : block * block_cells + block_cells + 2 * radius]
            for block in range(block_count)
        ],
        axis=3,
    )
    result = jnp.einsum("mlibk,kq->mlibq", windows, band_blocks, preferred_element_type=jnp.float32)
    return result.reshape(members_here, levels, lon_cells, lat_cells)


def pick_cells(field_rows, row_index, col_index, block_rows):
    row_count, col_count = field_rows.shape
    field_cols = field_rows.T

    def pick_one_block(indices):
        rows_here, cols_here = indices
        onehot_rows = (
            rows_here[:, None] == jnp.arange(row_count, dtype=jnp.int32)[None, :]
        ).astype(jnp.float32)
        onehot_cols = (
            cols_here[:, None] == jnp.arange(col_count, dtype=jnp.int32)[None, :]
        ).astype(jnp.float32)
        picked = jnp.dot(
            onehot_cols,
            field_cols,
            precision=lax.Precision.HIGHEST,
            preferred_element_type=jnp.float32,
        )
        return jnp.sum(picked * onehot_rows, axis=1)

    values = lax.map(
        pick_one_block, (row_index.reshape(-1, block_rows), col_index.reshape(-1, block_rows))
    )
    return values.reshape(-1)


def spread_cells(misfit, row_index, col_index, row_count, col_count, block_rows):

    def spread_one_block(total, items):
        rows_here, cols_here, values = items
        onehot_rows = (
            rows_here[:, None] == jnp.arange(row_count, dtype=jnp.int32)[None, :]
        ).astype(jnp.float32)
        onehot_cols = (
            cols_here[:, None] == jnp.arange(col_count, dtype=jnp.int32)[None, :]
        ).astype(jnp.float32)
        weighted = onehot_rows * values[:, None]
        return (
            total
            + jnp.dot(
                weighted.T,
                onehot_cols,
                precision=lax.Precision.HIGHEST,
                preferred_element_type=jnp.float32,
            ),
            None,
        )

    start = jnp.zeros((row_count, col_count), jnp.float32)
    items = (
        row_index.reshape(-1, block_rows),
        col_index.reshape(-1, block_rows),
        misfit.reshape(-1, block_rows),
    )
    total, _ = lax.scan(spread_one_block, start, items)
    return total


def local(control, perturb, lon_taps, lat_taps, innov, inv_var, cell_index, counts):
    members_here, levels, lon_cells, lat_cells = control.shape
    radius = lon_taps.shape[0] - 1
    block_cells = 144
    band_lon = lon_band(lon_taps, lon_cells)
    band_blocks = lat_block_band(lat_taps, block_cells)
    extended = extended_2(control, (("tile", 2),), radius)
    smoothed = localize(extended, band_lon, band_blocks, radius, block_cells)
    member_sum = jnp.sum(perturb.astype(jnp.float32) * smoothed, axis=0)
    slot_ids = lax.broadcasted_iota(jnp.int32, innov.shape, 2)
    is_live = slot_ids < counts[:, :, None]
    weights = jnp.where(is_live, inv_var, 0.0)
    received = (
        lax.all_to_all(innov, "tile", split_axis=1, concat_axis=0, tiled=True),
        lax.all_to_all(weights, "tile", split_axis=1, concat_axis=0, tiled=True),
        lax.all_to_all(cell_index, "tile", split_axis=1, concat_axis=0, tiled=True),
    )
    observed = received[0].reshape(-1)
    weight_recv = received[1].reshape(-1)
    cells_hit = received[2].reshape(-1)
    row_index = cells_hit // lat_cells
    col_index = cells_hit % lat_cells
    row_count = levels * lon_cells
    block_rows = math.gcd(observed.shape[0], 1024)
    increment = lax.psum(member_sum, "mem")
    at_cells = pick_cells(increment.reshape(row_count, lat_cells), row_index, col_index, block_rows)
    misfit = weight_recv * (at_cells - observed)
    spread = spread_cells(misfit, row_index, col_index, row_count, lat_cells, block_rows)
    spread = spread.reshape(levels, lon_cells, lat_cells)
    wide_pert = extended_2(perturb, (("tile", 2),), radius)
    wide_spread = extended_2(spread, (("tile", 1),), radius)
    wide_products = (wide_pert.astype(jnp.float32) * wide_spread[None]).astype(jnp.bfloat16)
    return control.astype(jnp.float32) + localize(
        wide_products, band_lon, band_blocks, radius, block_cells
    )


def solution(mesh):
    return jax.shard_map(
        local,
        mesh=mesh,
        in_specs=(
            P("mem", None, "tile", None),
            P("mem", None, "tile", None),
            P(),
            P(),
            P("tile", None, None),
            P("tile", None, None),
            P("tile", None, None),
            P("tile", None),
        ),
        out_specs=P("mem", None, "tile", None),
        check_vma=False,
    )
```

profile of v0, /device:TPU:11, one launch (start us, length us, event | category | flops | bytes accessed | tf_op | source)
XLA Modules:
  0.0 176.9 jit_solution(8008073635435257452)
XLA Ops:
  8.1 1.8 %collective-permute-start.2 = (bf16[20,1,16,720]{3,2,0,1:T(8,128)(2,1)S(1)}, bf16[20,1,16,720]{3,2,0,1:T(8,128)(2,1)}, u32[]{:S(2)}, u32[]{:S(2)}) collective-permute-start(bf16[20,1,16,720]{3,2,0,1:T(8,128)(2,1)S(1)} %get-tuple-element.115), channel_id=1, source_target_pairs={{0,4},{4,8},{8,12},{12,16},{16,20},{20,24},{24,28},{28,0},{1,5},{5... | collective-permute-start | bytes 1382408 | tf_op jit(solution)/shard_map/ppermute | solution.py:14
  11.2 4.9 %all-to-all-start = ((s32[1,8,256]{2,0,1:T(1,128)}), s32[1,8,256]{2,0,1:T(1,128)S(1)}, u32[]{:S(2)}, u32[]{:S(2)}) async-start(s32[1,8,256]{2,0,1:T(1,128)} %copy.48), calls=%async_computation | async-start | bytes 16384 | tf_op jit(solution)/shard_map/all_to_all | solution.py:136
  16.1 2.2 %fusion.167 = (bf16[20,1,16,720]{3,2,0,1:T(8,128)(2,1)}, bf16[20,1,16,720]{3,2,0,1:T(8,128)(2,1)S(1)}) fusion(bf16[20,1,45,720]{3,2,0,1:T(8,128)(2,1)} %bitcast.147), kind=kLoop, calls=%fused_computation.200 | loop fusion | bytes 1843200 | tf_op jit(solution)/shard_map/slice | solution.py:15
  23.2 4.4 %all-to-all-start.1 = ((f32[1,8,256]{2,0,1:T(1,128)}), f32[1,8,256]{2,0,1:T(1,128)S(1)}, u32[]{:S(2)}, u32[]{:S(2)}) async-start(f32[1,8,256]{2,0,1:T(1,128)} %compare_select_fusion), calls=%async_computation.1 | async-start | bytes 16384 | tf_op jit(solution)/shard_map/all_to_all | solution.py:135
  27.7 5.6 %all-to-all-done.1 = f32[1,8,256]{2,0,1:T(1,128)S(1)} async-done(((f32[1,8,256]{2,0,1:T(1,128)}), f32[1,8,256]{2,0,1:T(1,128)S(1)}, u32[]{:S(2)}, u32[]{:S(2)}) %all-to-all-start.1) | async-done | bytes 8224 | tf_op jit(solution)/shard_map/all_to_all | solution.py:135
  33.4 4.0 %all-to-all-start.2 = ((f32[1,8,256]{2,0,1:T(1,128)}), f32[1,8,256]{2,0,1:T(1,128)S(1)}, u32[]{:S(2)}, u32[]{:S(2)}) async-start(f32[1,8,256]{2,0,1:T(1,128)} %copy.57), calls=%async_computation.2 | async-start | bytes 16384 | tf_op jit(solution)/shard_map/all_to_all | solution.py:134
  37.5 3.1 %all-to-all-done.2 = f32[1,8,256]{2,0,1:T(1,128)S(1)} async-done(((f32[1,8,256]{2,0,1:T(1,128)}), f32[1,8,256]{2,0,1:T(1,128)S(1)}, u32[]{:S(2)}, u32[]{:S(2)}) %all-to-all-start.2) | async-done | bytes 8224 | tf_op jit(solution)/shard_map/all_to_all | solution.py:134
  40.7 12.1 %fusion.31 = bf16[20,1,45,720]{3,2,0,1:T(8,128)(2,1)S(1)} fusion(bf16[20,1,16,720]{3,2,0,1:T(8,128)(2,1)} %collective-permute-done.3, bf16[20,1,45,720]{3,2,0,1:T(8,128)(2,1)S(1)} %bitcast.146, bf16[20,1,16,720]{3,2,0,1:T(8,128)(2,1)} %collective-permute-done.2, f32[]{:T(128)} %bitcast.31, f32[]{:T(128)} %bitcast.30, f32[]{:T(128)} %bitcast.29, ...), kind=kOutput, calls=%fused_computation.44 | convolution fusion | flops 107279912 | bytes 3513668 | tf_op jit(solution)/shard_map/ij,mljk->mlik/dot_general | solution.py:46
  53.7 11.5 %fusion.25 = f32[20,45,5,144]{3,1,2,0:T(8,128)S(1)} fusion(f32[]{:T(128)} %bitcast.58, f32[]{:T(128)} %bitcast.57, f32[]{:T(128)} %bitcast.56, f32[]{:T(128)} %bitcast.55, f32[]{:T(128)} %bitcast.54, f32[]{:T(128)} %bitcast.53, f32[]{:T(128)} %bitcast.52, f32[]{:T(128)} %bitcast.51, f32[]{:T(128)} %bitcast.50, f32[]{:T(128)} %bitcast.49, f32[]{:T(128)} %bitcast.48, ...), kind=kOutput, calls=%fused_computation.38 | convolution fusion | flops 229439232 | bytes 4176772 | tf_op jit(solution)/shard_map/mlibk,kq->mlibq/dot_general | solution.py:59
  65.2 6.4 %copy.55 = f32[20,45,5,144]{3,2,1,0:T(8,128)} copy(f32[20,45,5,144]{3,1,2,0:T(8,128)S(1)} %fusion.25) | data formatting | bytes 5184000 | tf_op jit(solution)/shard_map/mlibk,kq->mlibq/dot_general | solution.py:59
  71.6 4.9 %reshape.136 = f32[20,1,45,720]{3,2,0,1:T(8,128)S(1)} reshape(f32[20,45,5,144]{3,2,1,0:T(8,128)} %copy.55) | data formatting | bytes 5184000 | tf_op jit(solution)/shard_map/reshape | solution.py:60
  76.4 2.4 %multiply_reduce_fusion = f32[45,720]{1,0:T(8,128)} fusion(f32[20,1,45,720]{3,2,0,1:T(8,128)S(1)} %reshape.136, bf16[20,1,45,720]{3,2,1,0:T(8,128)(2,1)} %param.13), kind=kLoop, calls=%fused_computation.22 | loop fusion | flops 1911600 | bytes 4017600 | tf_op jit(solution)/shard_map/reduce_sum | solution.py:129
  78.9 32.7 %all-reduce.4.cloned.1.call-done = f32[720,45]{0,1:T(8,128)} async-done(((f32[720,45]{0,1:T(8,128)}), f32[720,45]{0,1:T(8,128)}) %all-reduce.4.cloned.1.call-update) | async-done | bytes 129616 | tf_op jit(solution)/shard_map/psum | solution.py:145
  112.7 3.8 %while.21 = (s32[]{:T(128)}, f32[2,1024]{1,0:T(2,128)S(1)}, s32[2,1024]{1,0:T(2,128)S(1)}, s32[2,1024]{1,0:T(2,128)S(1)}, f32[720,45]{1,0:T(8,128)S(1)}, /*index=5*/s32[]{:T(128)}, s32[]{:T(128)}) while((s32[]{:T(128)}, f32[2,1024]{1,0:T(2,128)S(1)}, s32[2,1024]{1,0:T(2,128)S(1)}, s32[2,1024]{1,0:T(2,128)S(1)}, f32[720,45]{1,0:T(8,128)S(1)}, ...), condition=%wide.region_4.5_spmd, body=%wide.region_2.4_spmd.sunk | while | flops 399005696 | bytes 166549 | solution.py:83
  112.7 1.8 %fusion.179 = f32[1024]{0:T(1024)S(1)} fusion(f32[720,45]{1,0:T(8,128)S(1)} %get-tuple-element.245, s32[1024]{0:T(1024)S(1)} %bitcast.156, s32[1024]{0:T(1024)S(1)} %bitcast.157), kind=kOutput, calls=%fused_computation.4.clone.1 | convolution fusion | flops 399005696 | bytes 141888 | tf_op jit(solution)/shard_map/while/body/eval_jaxpr/dot_general | solution.py:75
  114.6 1.8 %fusion.179 = f32[1024]{0:T(1024)S(1)} fusion(f32[720,45]{1,0:T(8,128)S(1)} %get-tuple-element.245, s32[1024]{0:T(1024)S(1)} %bitcast.156, s32[1024]{0:T(1024)S(1)} %bitcast.157), kind=kOutput, calls=%fused_computation.4.clone.1 | convolution fusion | flops 399005696 | bytes 141888 | tf_op jit(solution)/shard_map/while/body/eval_jaxpr/dot_general | solution.py:75
  116.5 3.1 %while.22 = (s32[]{:T(128)}, f32[45,720]{1,0:T(8,128)S(1)}, s32[2,1024]{1,0:T(2,128)S(1)}, f32[2,1024]{1,0:T(2,128)S(1)}, s32[2,1024]{1,0:T(2,128)S(1)}, /*index=5*/s32[]{:T(128)}, s32[]{:T(128)}) while((s32[]{:T(128)}, f32[45,720]{1,0:T(8,128)S(1)}, s32[2,1024]{1,0:T(2,128)S(1)}, f32[2,1024]{1,0:T(2,128)S(1)}, ...), condition=%wide.region_6.7_spmd.clone, body=%wide.region_5.6_spmd.clone.sunk | while | flops 399025440 | bytes 296159 | solution.py:117
  119.7 3.9 %collective-permute-start.4 = (f32[1,16,720]{2,1,0:T(8,128)S(1)}, f32[1,16,720]{2,1,0:T(8,128)S(1)}, u32[]{:S(2)}, u32[]{:S(2)}) collective-permute-start(f32[1,16,720]{2,1,0:T(8,128)S(1)} %get-tuple-element.119), channel_id=1, source_target_pairs={{0,4},{4,8},{8,12},{12,16},{16,20},{20,24},{24,28},{28,0},{1,5},{5... | collective-permute-start | bytes 138248 | tf_op jit(solution)/shard_map/ppermute | solution.py:14
  124.7 3.2 %collective-permute-done.5 = f32[1,16,720]{2,1,0:T(8,128)S(1)} collective-permute-done((f32[1,16,720]{2,1,0:T(8,128)S(1)}, f32[1,16,720]{2,1,0:T(8,128)S(1)}, u32[]{:S(2)}, u32[]{:S(2)}) %collective-permute-start.5) | collective-permute-done | bytes 46112 | tf_op jit(solution)/shard_map/ppermute | solution.py:17
  128.0 12.3 %fusion.30 = bf16[20,1,45,720]{3,2,0,1:T(8,128)(2,1)S(1)} fusion(bf16[20,16,720]{2,1,0:T(8,128)(2,1)} %bitcast.8, bf16[20,45,720]{2,1,0:T(8,128)(2,1)S(1)} %bitcast.148, bf16[20,16,720]{2,1,0:T(8,128)(2,1)} %bitcast.5, f32[77,720]{1,0:T(8,128)S(1)} %maximum_bitcast_fusion.6, f32[]{:T(128)} %bitcast.31, f32[]{:T(128)} %bitcast.30, f32[]{:T(128)} %bitcast.29, ...), kind=kOutput, calls=%fused_computation.43 | convolution fusion | flops 109497512 | bytes 3735428 | tf_op jit(solution)/shard_map/ij,mljk->mlik/dot_general | solution.py:46
  141.2 11.5 %fusion.23 = f32[20,45,5,144]{3,1,2,0:T(8,128)S(1)} fusion(f32[]{:T(128)} %bitcast.58, f32[]{:T(128)} %bitcast.57, f32[]{:T(128)} %bitcast.56, f32[]{:T(128)} %bitcast.55, f32[]{:T(128)} %bitcast.54, f32[]{:T(128)} %bitcast.53, f32[]{:T(128)} %bitcast.52, f32[]{:T(128)} %bitcast.51, f32[]{:T(128)} %bitcast.50, f32[]{:T(128)} %bitcast.49, f32[]{:T(128)} %bitcast.48, ...), kind=kOutput, calls=%fused_computation.36 | convolution fusion | flops 229439232 | bytes 4176772 | tf_op jit(solution)/shard_map/mlibk,kq->mlibq/dot_general | solution.py:59
  152.7 6.4 %copy.59 = f32[20,45,5,144]{3,2,1,0:T(8,128)} copy(f32[20,45,5,144]{3,1,2,0:T(8,128)S(1)} %fusion.23) | data formatting | bytes 5184000 | tf_op jit(solution)/shard_map/mlibk,kq->mlibq/dot_general | solution.py:59
  159.1 4.9 %reshape.141 = f32[20,1,45,720]{3,2,0,1:T(8,128)S(1)} reshape(f32[20,45,5,144]{3,2,1,0:T(8,128)} %copy.59) | data formatting | bytes 5184000 | tf_op jit(solution)/shard_map/reshape | solution.py:60
  165.7 4.4 %copy.60 = f32[20,1,45,720]{3,1,2,0:T(1,128)} copy(f32[20,1,45,720]{3,2,0,1:T(8,128)S(1)} %convert_add_fusion) | data formatting | bytes 5184000 | tf_op jit(solution)/shard_map/add | solution.py:153
  (72 shorter events, 16.9 us)
Async XLA Ops:
  6.5 34.1 %copy-start = (bf16[20,1,45,720]{3,2,1,0:T(8,128)(2,1)S(1)}, bf16[20,1,45,720]{3,2,1,0:T(8,128)(2,1)}, u32[]{:S(2)}) copy-start(bf16[20,1,45,720]{3,2,1,0:T(8,128)(2,1)} %param.12) | copy-start | bytes 3888004
  6.5 13.2 %copy-start.7 = (s32[1,8]{1,0:T(1,128)S(1)}, s32[1,8]{1,0:T(1,128)}, u32[]{:S(2)}) copy-start(s32[1,8]{1,0:T(1,128)} %param.19) | copy-start | bytes 100
  6.5 13.2 %copy-start.5 = (f32[1,8,256]{2,1,0:T(8,128)S(1)}, f32[1,8,256]{2,1,0:T(8,128)}, u32[]{:S(2)}) copy-start(f32[1,8,256]{2,1,0:T(8,128)} %param.17) | copy-start | bytes 24580
  6.5 13.9 %copy-start.3 = (bf16[17]{0:T(256)(128)(2,1)S(1)}, bf16[17]{0:T(256)(128)(2,1)}, u32[]{:S(2)}) copy-start(bf16[17]{0:T(256)(128)(2,1)} %param.14) | copy-start | bytes 106
  6.5 14.6 %copy-start.4 = (bf16[17]{0:T(256)(128)(2,1)S(1)}, bf16[17]{0:T(256)(128)(2,1)}, u32[]{:S(2)}) copy-start(bf16[17]{0:T(256)(128)(2,1)} %param.15) | copy-start | bytes 106
  6.5 15.3 %copy-start.6 = (f32[1,8,256]{2,1,0:T(8,128)S(1)}, f32[1,8,256]{2,1,0:T(8,128)}, u32[]{:S(2)}) copy-start(f32[1,8,256]{2,1,0:T(8,128)} %param.16) | copy-start | bytes 24580
  8.1 32.6 %collective-permute-start.2 = (bf16[20,1,16,720]{3,2,0,1:T(8,128)(2,1)S(1)}, bf16[20,1,16,720]{3,2,0,1:T(8,128)(2,1)}, u32[]{:S(2)}, u32[]{:S(2)}) collective-permute-start(bf16[20,1,16,720]{3,2,0,1:T(8,128)(2,1)S(1)} %get-tuple-element.115), channel_id=1, source_target_pairs={{0,4},{4,8},{8,12},{12,16},{16,20},{20,24},{24,28},{28,0},{1,5},{5... | collective-permute-start | bytes 1382408 | tf_op jit(solution)/shard_map/ppermute | solution.py:14
  9.9 30.7 %collective-permute-start.3 = (bf16[20,1,16,720]{3,2,0,1:T(8,128)(2,1)S(1)}, bf16[20,1,16,720]{3,2,0,1:T(8,128)(2,1)}, u32[]{:S(2)}, u32[]{:S(2)}) collective-permute-start(bf16[20,1,16,720]{3,2,0,1:T(8,128)(2,1)S(1)} %get-tuple-element.116), channel_id=1, source_target_pairs={{4,0},{8,4},{12,8},{16,12},{20,16},{24,20},{28,24},{0,28},{5,1},{9... | collective-permute-start | bytes 1382408 | tf_op jit(solution)/shard_map/ppermute | solution.py:17
  11.2 12.0 %all-to-all-start = ((s32[1,8,256]{2,0,1:T(1,128)}), s32[1,8,256]{2,0,1:T(1,128)S(1)}, u32[]{:S(2)}, u32[]{:S(2)}) async-start(s32[1,8,256]{2,0,1:T(1,128)} %copy.48), calls=%async_computation | async-start | bytes 16384 | tf_op jit(solution)/shard_map/all_to_all | solution.py:136
  18.3 109.7 %collective-permute-start = (bf16[20,1,16,720]{3,2,0,1:T(8,128)(2,1)}, bf16[20,1,16,720]{3,2,0,1:T(8,128)(2,1)}, u32[]{:S(2)}, u32[]{:S(2)}) collective-permute-start(bf16[20,1,16,720]{3,2,0,1:T(8,128)(2,1)} %get-tuple-element.117), channel_id=1, source_target_pairs={{0,4},{4,8},{8,12},{12,16},{16,20},{20,24},{24,28},{28,0},{1,5},{5... | collective-permute-start | bytes 1382408 | tf_op jit(solution)/shard_map/ppermute | solution.py:14
  19.8 108.2 %collective-permute-start.1 = (bf16[20,1,16,720]{3,2,0,1:T(8,128)(2,1)S(1)}, bf16[20,1,16,720]{3,2,0,1:T(8,128)(2,1)}, u32[]{:S(2)}, u32[]{:S(2)}) collective-permute-start(bf16[20,1,16,720]{3,2,0,1:T(8,128)(2,1)S(1)} %get-tuple-element.118), channel_id=1, source_target_pairs={{4,0},{8,4},{12,8},{16,12},{20,16},{24,20},{28,24},{0,28},{5,1},{9... | collective-permute-start | bytes 1382408 | tf_op jit(solution)/shard_map/ppermute | solution.py:17
  23.2 10.1 %all-to-all-start.1 = ((f32[1,8,256]{2,0,1:T(1,128)}), f32[1,8,256]{2,0,1:T(1,128)S(1)}, u32[]{:S(2)}, u32[]{:S(2)}) async-start(f32[1,8,256]{2,0,1:T(1,128)} %compare_select_fusion), calls=%async_computation.1 | async-start | bytes 16384 | tf_op jit(solution)/shard_map/all_to_all | solution.py:135
  33.4 7.2 %all-to-all-start.2 = ((f32[1,8,256]{2,0,1:T(1,128)}), f32[1,8,256]{2,0,1:T(1,128)S(1)}, u32[]{:S(2)}, u32[]{:S(2)}) async-start(f32[1,8,256]{2,0,1:T(1,128)} %copy.57), calls=%async_computation.2 | async-start | bytes 16384 | tf_op jit(solution)/shard_map/all_to_all | solution.py:134
  37.3 74.3 %all-reduce.4.cloned.1.call-start = ((), (), s32[]{:S(2)}) async-start(), calls=%async_computation.3 | async-start | bytes 294912 | tf_op jit(solution)/shard_map/psum | solution.py:145
  112.7 3.8 %copy-start.2 = (f32[45,720]{1,0:T(8,128)S(1)}, f32[45,720]{1,0:T(8,128)}, u32[]{:S(2)}) copy-start(f32[45,720]{1,0:T(8,128)} %custom-call) | copy-start | bytes 388804
  116.5 11.5 %copy-start.1 = (bf16[20,1,45,720]{3,2,1,0:T(8,128)(2,1)S(1)}, bf16[20,1,45,720]{3,2,1,0:T(8,128)(2,1)}, u32[]{:S(2)}) copy-start(bf16[20,1,45,720]{3,2,1,0:T(8,128)(2,1)} %param.13) | copy-start | bytes 3888004
  119.7 5.1 %collective-permute-start.4 = (f32[1,16,720]{2,1,0:T(8,128)S(1)}, f32[1,16,720]{2,1,0:T(8,128)S(1)}, u32[]{:S(2)}, u32[]{:S(2)}) collective-permute-start(f32[1,16,720]{2,1,0:T(8,128)S(1)} %get-tuple-element.119), channel_id=1, source_target_pairs={{0,4},{4,8},{8,12},{12,16},{16,20},{20,24},{24,28},{28,0},{1,5},{5... | collective-permute-start | bytes 138248 | tf_op jit(solution)/shard_map/ppermute | solution.py:14
  123.5 4.4 %collective-permute-start.5 = (f32[1,16,720]{2,1,0:T(8,128)S(1)}, f32[1,16,720]{2,1,0:T(8,128)S(1)}, u32[]{:S(2)}, u32[]{:S(2)}) collective-permute-start(f32[1,16,720]{2,1,0:T(8,128)S(1)} %get-tuple-element.120), channel_id=1, source_target_pairs={{4,0},{8,4},{12,8},{16,12},{20,16},{24,20},{28,24},{0,28},{5,1},{9... | collective-permute-start | bytes 138248 | tf_op jit(solution)/shard_map/ppermute | solution.py:17
Sparse Core Ops, SparseCore 0:
  79.0 32.5 all-reduce.3
where the time goes:
time: 178 us; the launch traced here: 177 us
  matrix products  54 us (30%)
  waiting for transfers between devices  46.7 us (26%)
  local copies, waits for them, and re-layouts  37 us (21%)
  starting transfers between devices  20.5 us (12%)
  between operations  13.7 us (8%)
  other arithmetic  4.93 us (3%)
    psum x1, waiting for transfers between devices, local(): increment = lax.psum(member_sum, 'mem')  32.7 us
    dot_general x2, matrix products, localize(): jnp.einsum('ij,mljk->mlik', band_lon, extended, preferred_element_type=jn...  24.4 us
    dot_general x2, matrix products, localize(): jnp.einsum('mlibk,kq->mlibq', windows, band_blocks, preferred_element_typ...  23 us
    dot_general x2, local copies, waits for them, and re-layouts, localize(): jnp.einsum('mlibk,kq->mlibq', windows, band_blocks, preferred_element_typ...  12.8 us
    reshape x2, local copies, waits for them, and re-layouts, localize(): return result.reshape(members_here, levels, lon_cells, lat_cells)  9.75 us
    ppermute x3, starting transfers between devices, extended_2(): lax.ppermute(lax.slice_in_dim(block, block.shape[dim] - width, None, axis...  7.17 us
    all_to_all x1, waiting for transfers between devices, local(): lax.all_to_all(weights, 'tile', split_axis=1, concat_axis=0, tiled=True)  5.65 us
    all_to_all x1, starting transfers between devices, local(): lax.all_to_all(cell_index, 'tile', split_axis=1, concat_axis=0, tiled=True)  4.92 us
  transfers between devices with their start and end apart: 10, of which 6 were waited for; matrix products, arithmetic and copies ran while one was open for 30% of the time, Pallas kernels for 0%

commit v1 on v0

--- a/solution.py
+++ b/solution.py
@@ -3,6 +3,29 @@
 import jax.numpy as jnp
 from jax import lax
 from jax.sharding import PartitionSpec as P
+
+
+def cut_along(value, dim, size):
+    shape = value.shape
+    blocks = value.reshape(*shape[:dim], size, shape[dim] // size, *shape[dim + 1 :])
+    return jnp.moveaxis(blocks, dim, 0)
+
+
+def joined_along(blocks, dim):
+    blocks = jnp.moveaxis(blocks, 0, dim)
+    dims = blocks.shape
+    return blocks.reshape(*dims[:dim], dims[dim] * dims[dim + 1], *dims[dim + 2 :])
+
+
+def swapped_with_each(x, axis, split_dim, concat_dim):
+    devices, index = (lax.axis_size(axis), lax.axis_index(axis))
+    parts = cut_along(x, split_dim, devices)
+    outs = [parts[index]]
+    for hop in range(1, devices):
+        sent = parts[index ^ hop]
+        outs.append(lax.ppermute(sent, axis, [(i, i ^ hop) for i in range(devices)]))
+    parts = jnp.stack(outs)[index ^ jnp.arange(devices)]
+    return joined_along(parts, concat_dim)
 
 
 def extended_2(block, sides, width):
@@ -133,7 +156,7 @@
     received = (
         lax.all_to_all(innov, "tile", split_axis=1, concat_axis=0, tiled=True),
         lax.all_to_all(weights, "tile", split_axis=1, concat_axis=0, tiled=True),
-        lax.all_to_all(cell_index, "tile", split_axis=1, concat_axis=0, tiled=True),
+        swapped_with_each(cell_index, "tile", 1, 0),
     )
     observed = received[0].reshape(-1)
     weight_recv = received[1].reshape(-1)

time: 178 us -> 174 us (0.978)
  waiting for transfers between devices: 46.7 us -> 36.6 us
  local copies, waits for them, and re-layouts: 37 us -> 39.8 us
  starting transfers between devices: 20.5 us -> 22.7 us
    psum x1, waiting for transfers between devices: 32.7 us -> 26 us  [local(): increment = lax.psum(member_sum, 'mem')]
    ppermute x0 -> x7, starting transfers between devices: none -> 6.23 us  [swapped_with_each(): lax.ppermute(sent, axis, [(i, i ^ hop) for i in range(devices)])]
    all_to_all x1, waiting for transfers between devices: 5.65 us -> 0.01 us  [local(): lax.all_to_all(weights, 'tile', split_axis=1, concat_axis=0, tiled=True)]
    all_to_all x1 -> x0, starting transfers between devices: 4.92 us -> none  [local(): lax.all_to_all(cell_index, 'tile', split_axis=1, concat_axis=0, tiled=True)]
    ppermute x0 -> x7, waiting for transfers between devices: none -> 2.92 us  [swapped_with_each(): lax.ppermute(sent, axis, [(i, i ^ hop) for i in range(devices)])]
    slice x2, local copies, waits for them, and re-layouts: 1.41 us -> 3.97 us  [band_from(): band = band + jnp.where(offsets == offset, taps[offset], 0.0)]
  transfers between devices with their start and end apart: 10 -> 16, of which waited for: 6 -> 5; matrix products, arithmetic and copies ran while one was open for 30% -> 32% of each run, Pallas kernels for 0% -> 0%
where the time goes in v1:
time: 174 us; the launch traced here: 173 us
  matrix products  54.3 us (31%)
  local copies, waits for them, and re-layouts  39.8 us (23%)
  waiting for transfers between devices  36.6 us (21%)
  starting transfers between devices  22.7 us (13%)
  between operations  13.7 us (8%)
  other arithmetic  5.55 us (3%)
    psum x1, waiting for transfers between devices, local(): increment = lax.psum(member_sum, 'mem')  26 us
    dot_general x2, matrix products, localize(): jnp.einsum('ij,mljk->mlik', band_lon, extended, preferred_element_type=jn...  25.2 us
    dot_general x2, matrix products, localize(): jnp.einsum('mlibk,kq->mlibq', windows, band_blocks, preferred_element_typ...  22.6 us
    dot_general x2, local copies, waits for them, and re-layouts, localize(): jnp.einsum('mlibk,kq->mlibq', windows, band_blocks, preferred_element_typ...  12.8 us
    reshape x2, local copies, waits for them, and re-layouts, localize(): return result.reshape(members_here, levels, lon_cells, lat_cells)  9.75 us
    ppermute x3, starting transfers between devices, extended_2(): lax.ppermute(lax.slice_in_dim(block, block.shape[dim] - width, None, axis...  6.53 us
    ppermute x7, starting transfers between devices, swapped_with_each(): lax.ppermute(sent, axis, [(i, i ^ hop) for i in range(devices)])  6.23 us
    all_to_all x1, starting transfers between devices, local(): lax.all_to_all(innov, 'tile', split_axis=1, concat_axis=0, tiled=True)  4.97 us
  transfers between devices with their start and end apart: 16, of which 5 were waited for; matrix products, arithmetic and copies ran while one was open for 32% of the time, Pallas kernels for 0%

profile of v1, /device:TPU:11, one launch (start us, length us, event | category | flops | bytes accessed | tf_op | source)
XLA Modules:
  0.0 172.8 jit_solution(12992460935596948629)
XLA Ops:
  9.9 2.1 %collective-permute-start.3 = (s32[1,1,256]{2,1,0:T(1,128)S(1)}, s32[1,1,256]{2,1,0:T(1,128)S(1)}, u32[]{:S(2)}, u32[]{:S(2)}) collective-permute-start(s32[1,1,256]{2,1,0:T(1,128)S(1)} %get-tuple-element.127), channel_id=1, source_target_pairs={{0,8},{4,12},{8,0},{12,4},{16,24},{20,28},{24,16},{28,20},{1,9},{5... | collective-permute-start | bytes 3080 | tf_op jit(solution)/shard_map/ppermute | solution.py:26
  14.6 4.2 %all-to-all-start = ((f32[1,8,256]{2,0,1:T(1,128)}), f32[1,8,256]{2,0,1:T(1,128)S(1)}, u32[]{:S(2)}, u32[]{:S(2)}) async-start(f32[1,8,256]{2,0,1:T(1,128)} %compare_select_fusion), calls=%async_computation | async-start | bytes 16384 | tf_op jit(solution)/shard_map/all_to_all | solution.py:158
  18.9 2.0 %fusion.172 = (f32[1]{0:T(128)}, f32[1]{0:T(128)}, f32[1]{0:T(128)}, f32[1]{0:T(128)}, f32[1]{0:T(128)}, /*index=5*/f32[1]{0:T(128)}, f32[1]{0:T(128)}, f32[1]{0...) fusion(bf16[17]{0:T(256)(128)(2,1)} %param.14), kind=kLoop, calls=%fused_computation.216 | loop fusion | bytes 136 | tf_op jit(solution)/shard_map/slice | solution.py:50
  20.9 2.0 %fusion.171 = (f32[1]{0:T(128)}, f32[1]{0:T(128)}, f32[1]{0:T(128)}, f32[1]{0:T(128)}, f32[1]{0:T(128)}, /*index=5*/f32[1]{0:T(128)}, f32[1]{0:T(128)}, f32[1]{0...) fusion(bf16[17]{0:T(256)(128)(2,1)} %param.15), kind=kLoop, calls=%fused_computation.215 | loop fusion | bytes 136 | tf_op jit(solution)/shard_map/slice | solution.py:50
  22.8 2.2 %fusion.169 = (bf16[20,1,16,720]{3,2,0,1:T(8,128)(2,1)}, bf16[20,1,16,720]{3,2,0,1:T(8,128)(2,1)S(1)}) fusion(bf16[20,1,45,720]{3,2,0,1:T(8,128)(2,1)} %bitcast.159), kind=kLoop, calls=%fused_computation.213 | loop fusion | bytes 1843200 | tf_op jit(solution)/shard_map/slice | solution.py:38
  31.1 2.9 %collective-permute-done.7 = s32[1,1,256]{2,1,0:T(1,128)S(1)} collective-permute-done((s32[1,1,256]{2,1,0:T(1,128)S(1)}, s32[1,1,256]{2,1,0:T(1,128)S(1)}, u32[]{:S(2)}, u32[]{:S(2)}) %collective-permute-start.7) | collective-permute-done | bytes 1056 | tf_op jit(solution)/shard_map/ppermute | solution.py:26
  34.7 12.5 %fusion.31 = bf16[20,1,45,720]{3,2,0,1:T(8,128)(2,1)S(1)} fusion(bf16[20,1,16,720]{3,2,0,1:T(8,128)(2,1)} %collective-permute-done.10, bf16[20,1,45,720]{3,2,0,1:T(8,128)(2,1)S(1)} %bitcast.158, bf16[20,1,16,720]{3,2,0,1:T(8,128)(2,1)} %collective-permute-done.9, f32[]{:T(128)} %bitcast.41, f32[]{:T(128)} %bitcast.40, f32[]{:T(128)} %bitcast.39, ...), kind=kOutput, calls=%fused_computation.45 | convolution fusion | flops 107279912 | bytes 3513668 | tf_op jit(solution)/shard_map/ij,mljk->mlik/dot_general | solution.py:69
  48.1 11.3 %fusion.25 = f32[20,45,5,144]{3,1,2,0:T(8,128)S(1)} fusion(f32[]{:T(128)} %bitcast.68, f32[]{:T(128)} %bitcast.67, f32[]{:T(128)} %bitcast.66, f32[]{:T(128)} %bitcast.65, f32[]{:T(128)} %bitcast.64, f32[]{:T(128)} %bitcast.63, f32[]{:T(128)} %bitcast.62, f32[]{:T(128)} %bitcast.61, f32[]{:T(128)} %bitcast.60, f32[]{:T(128)} %bitcast.59, f32[]{:T(128)} %bitcast.58, ...), kind=kOutput, calls=%fused_computation.39 | convolution fusion | flops 229439232 | bytes 4176772 | tf_op jit(solution)/shard_map/mlibk,kq->mlibq/dot_general | solution.py:82
  59.4 6.4 %copy.53 = f32[20,45,5,144]{3,2,1,0:T(8,128)} copy(f32[20,45,5,144]{3,1,2,0:T(8,128)S(1)} %fusion.25) | data formatting | bytes 5184000 | tf_op jit(solution)/shard_map/mlibk,kq->mlibq/dot_general | solution.py:82
  65.8 4.9 %reshape.162 = f32[20,1,45,720]{3,2,0,1:T(8,128)S(1)} reshape(f32[20,45,5,144]{3,2,1,0:T(8,128)} %copy.53) | data formatting | bytes 5184000 | tf_op jit(solution)/shard_map/reshape | solution.py:83
  70.6 2.4 %multiply_reduce_fusion = f32[45,720]{1,0:T(8,128)} fusion(f32[20,1,45,720]{3,2,0,1:T(8,128)S(1)} %reshape.162, bf16[20,1,45,720]{3,2,1,0:T(8,128)(2,1)} %param.13), kind=kLoop, calls=%fused_computation.23 | loop fusion | flops 1911600 | bytes 4017600 | tf_op jit(solution)/shard_map/reduce_sum | solution.py:152
  73.1 5.0 %all-to-all-start.1 = ((f32[1,8,256]{2,0,1:T(1,128)}), f32[1,8,256]{2,0,1:T(1,128)S(1)}, u32[]{:S(2)}, u32[]{:S(2)}) async-start(f32[1,8,256]{2,0,1:T(1,128)} %copy.55), calls=%async_computation.1 | async-start | bytes 16384 | tf_op jit(solution)/shard_map/all_to_all | solution.py:157
  78.1 3.2 %all-to-all-done.1 = f32[1,8,256]{2,0,1:T(1,128)S(1)} async-done(((f32[1,8,256]{2,0,1:T(1,128)}), f32[1,8,256]{2,0,1:T(1,128)S(1)}, u32[]{:S(2)}, u32[]{:S(2)}) %all-to-all-start.1) | async-done | bytes 8224 | tf_op jit(solution)/shard_map/all_to_all | solution.py:157
  81.3 26.0 %all-reduce.4.cloned.1.call-done = f32[720,45]{0,1:T(8,128)} async-done(((f32[720,45]{0,1:T(8,128)}), f32[720,45]{0,1:T(8,128)}) %all-reduce.4.cloned.1.call-update) | async-done | bytes 129616 | tf_op jit(solution)/shard_map/psum | solution.py:168
  108.4 3.8 %while.21 = (s32[]{:T(128)}, f32[2,1024]{1,0:T(2,128)S(1)}, s32[2,1024]{1,0:T(2,128)S(1)}, s32[2,1024]{1,0:T(2,128)S(1)}, f32[720,45]{1,0:T(8,128)S(1)}, /*index=5*/s32[]{:T(128)}, s32[]{:T(128)}) while((s32[]{:T(128)}, f32[2,1024]{1,0:T(2,128)S(1)}, s32[2,1024]{1,0:T(2,128)S(1)}, s32[2,1024]{1,0:T(2,128)S(1)}, f32[720,45]{1,0:T(8,128)S(1)}, ...), condition=%wide.region_4.5_spmd, body=%wide.region_2.4_spmd.sunk | while | flops 399005696 | bytes 166549 | solution.py:106
  108.5 1.8 %fusion.181 = f32[1024]{0:T(1024)S(1)} fusion(f32[720,45]{1,0:T(8,128)S(1)} %get-tuple-element.253, s32[1024]{0:T(1024)S(1)} %bitcast.169, s32[1024]{0:T(1024)S(1)} %bitcast.170), kind=kOutput, calls=%fused_computation.5.clone.1 | convolution fusion | flops 399005696 | bytes 141888 | tf_op jit(solution)/shard_map/while/body/eval_jaxpr/dot_general | solution.py:98
  112.3 3.1 %while.22 = (s32[]{:T(128)}, f32[45,720]{1,0:T(8,128)S(1)}, s32[2,1024]{1,0:T(2,128)S(1)}, f32[2,1024]{1,0:T(2,128)S(1)}, s32[2,1024]{1,0:T(2,128)S(1)}, /*index=5*/s32[]{:T(128)}, s32[]{:T(128)}) while((s32[]{:T(128)}, f32[45,720]{1,0:T(8,128)S(1)}, s32[2,1024]{1,0:T(2,128)S(1)}, f32[2,1024]{1,0:T(2,128)S(1)}, ...), condition=%wide.region_6.7_spmd.clone, body=%wide.region_5.6_spmd.clone.sunk | while | flops 399025440 | bytes 296159 | solution.py:140
  115.4 3.9 %collective-permute-start.11 = (f32[1,16,720]{2,1,0:T(8,128)S(1)}, f32[1,16,720]{2,1,0:T(8,128)S(1)}, u32[]{:S(2)}, u32[]{:S(2)}) collective-permute-start(f32[1,16,720]{2,1,0:T(8,128)S(1)} %get-tuple-element.117), channel_id=1, source_target_pairs={{0,4},{4,8},{8,12},{12,16},{16,20},{20,24},{24,28},{28,0},{1,5},{5... | collective-permute-start | bytes 138248 | tf_op jit(solution)/shard_map/ppermute | solution.py:37
  120.5 3.2 %collective-permute-done.12 = f32[1,16,720]{2,1,0:T(8,128)S(1)} collective-permute-done((f32[1,16,720]{2,1,0:T(8,128)S(1)}, f32[1,16,720]{2,1,0:T(8,128)S(1)}, u32[]{:S(2)}, u32[]{:S(2)}) %collective-permute-start.12) | collective-permute-done | bytes 46112 | tf_op jit(solution)/shard_map/ppermute | solution.py:40
  123.8 12.7 %fusion.30 = bf16[20,1,45,720]{3,2,0,1:T(8,128)(2,1)S(1)} fusion(bf16[20,16,720]{2,1,0:T(8,128)(2,1)} %bitcast.8, bf16[20,45,720]{2,1,0:T(8,128)(2,1)S(1)} %bitcast.160, bf16[20,16,720]{2,1,0:T(8,128)(2,1)} %bitcast.5, f32[77,720]{1,0:T(8,128)S(1)} %maximum_bitcast_fusion.6, f32[]{:T(128)} %bitcast.41, f32[]{:T(128)} %bitcast.40, f32[]{:T(128)} %bitcast.39, ...), kind=kOutput, calls=%fused_computation.44 | convolution fusion | flops 109497512 | bytes 3735428 | tf_op jit(solution)/shard_map/ij,mljk->mlik/dot_general | solution.py:69
  137.4 11.3 %fusion.23 = f32[20,45,5,144]{3,1,2,0:T(8,128)S(1)} fusion(f32[]{:T(128)} %bitcast.68, f32[]{:T(128)} %bitcast.67, f32[]{:T(128)} %bitcast.66, f32[]{:T(128)} %bitcast.65, f32[]{:T(128)} %bitcast.64, f32[]{:T(128)} %bitcast.63, f32[]{:T(128)} %bitcast.62, f32[]{:T(128)} %bitcast.61, f32[]{:T(128)} %bitcast.60, f32[]{:T(128)} %bitcast.59, f32[]{:T(128)} %bitcast.58, ...), kind=kOutput, calls=%fused_computation.37 | convolution fusion | flops 229439232 | bytes 4176772 | tf_op jit(solution)/shard_map/mlibk,kq->mlibq/dot_general | solution.py:82
  148.6 6.4 %copy.57 = f32[20,45,5,144]{3,2,1,0:T(8,128)} copy(f32[20,45,5,144]{3,1,2,0:T(8,128)S(1)} %fusion.23) | data formatting | bytes 5184000 | tf_op jit(solution)/shard_map/mlibk,kq->mlibq/dot_general | solution.py:82
  155.0 4.9 %reshape.167 = f32[20,1,45,720]{3,2,0,1:T(8,128)S(1)} reshape(f32[20,45,5,144]{3,2,1,0:T(8,128)} %copy.57) | data formatting | bytes 5184000 | tf_op jit(solution)/shard_map/reshape | solution.py:83
  161.6 4.4 %copy.58 = f32[20,1,45,720]{3,1,2,0:T(1,128)} copy(f32[20,1,45,720]{3,2,0,1:T(8,128)S(1)} %convert_add_fusion) | data formatting | bytes 5184000 | tf_op jit(solution)/shard_map/add | solution.py:176
  (80 shorter events, 23.5 us)
Async XLA Ops:
  6.5 28.2 %copy-start = (bf16[20,1,45,720]{3,2,1,0:T(8,128)(2,1)S(1)}, bf16[20,1,45,720]{3,2,1,0:T(8,128)(2,1)}, u32[]{:S(2)}) copy-start(bf16[20,1,45,720]{3,2,1,0:T(8,128)(2,1)} %param.12) | copy-start | bytes 3888004
  6.5 22.8 %copy-start.3 = (f32[1,8,256]{2,1,0:T(8,128)S(1)}, f32[1,8,256]{2,1,0:T(8,128)}, u32[]{:S(2)}) copy-start(f32[1,8,256]{2,1,0:T(8,128)} %param.16) | copy-start | bytes 24580
  8.1 26.6 %collective-permute-start.10 = (bf16[20,1,16,720]{3,2,0,1:T(8,128)(2,1)S(1)}, bf16[20,1,16,720]{3,2,0,1:T(8,128)(2,1)}, u32[]{:S(2)}, u32[]{:S(2)}) collective-permute-start(bf16[20,1,16,720]{3,2,0,1:T(8,128)(2,1)S(1)} %get-tuple-element.114), channel_id=1, source_target_pairs={{4,0},{8,4},{12,8},{16,12},{20,16},{24,20},{28,24},{0,28},{5,1},{9... | collective-permute-start | bytes 1382408 | tf_op jit(solution)/shard_map/ppermute | solution.py:40
  9.8 15.2 %collective-permute-start.2 = (s32[1,1,256]{2,1,0:T(1,128)S(1)}, s32[1,1,256]{2,1,0:T(1,128)S(1)}, u32[]{:S(2)}, u32[]{:S(2)}) collective-permute-start(s32[1,1,256]{2,1,0:T(1,128)S(1)} %get-tuple-element.128), channel_id=1, source_target_pairs={{0,4},{4,0},{8,12},{12,8},{16,20},{20,16},{24,28},{28,24},{1,5},{5... | collective-permute-start | bytes 3080 | tf_op jit(solution)/shard_map/ppermute | solution.py:26
  9.9 16.6 %collective-permute-start.3 = (s32[1,1,256]{2,1,0:T(1,128)S(1)}, s32[1,1,256]{2,1,0:T(1,128)S(1)}, u32[]{:S(2)}, u32[]{:S(2)}) collective-permute-start(s32[1,1,256]{2,1,0:T(1,128)S(1)} %get-tuple-element.127), channel_id=1, source_target_pairs={{0,8},{4,12},{8,0},{12,4},{16,24},{20,28},{24,16},{28,20},{1,9},{5... | collective-permute-start | bytes 3080 | tf_op jit(solution)/shard_map/ppermute | solution.py:26
  12.0 14.7 %collective-permute-start.4 = (s32[1,1,256]{2,1,0:T(1,128)S(1)}, s32[1,1,256]{2,1,0:T(1,128)S(1)}, u32[]{:S(2)}, u32[]{:S(2)}) collective-permute-start(s32[1,1,256]{2,1,0:T(1,128)S(1)} %get-tuple-element.126), channel_id=1, source_target_pairs={{0,12},{4,8},{8,4},{12,0},{16,28},{20,24},{24,20},{28,16},{1,13},{... | collective-permute-start | bytes 3080 | tf_op jit(solution)/shard_map/ppermute | solution.py:26
  12.0 15.8 %collective-permute-start.5 = (s32[1,1,256]{2,1,0:T(1,128)S(1)}, s32[1,1,256]{2,1,0:T(1,128)S(1)}, u32[]{:S(2)}, u32[]{:S(2)}) collective-permute-start(s32[1,1,256]{2,1,0:T(1,128)S(1)} %get-tuple-element.125), channel_id=1, source_target_pairs={{0,16},{4,20},{8,24},{12,28},{16,0},{20,4},{24,8},{28,12},{1,17},{... | collective-permute-start | bytes 3080 | tf_op jit(solution)/shard_map/ppermute | solution.py:26
  14.6 58.4 %all-to-all-start = ((f32[1,8,256]{2,0,1:T(1,128)}), f32[1,8,256]{2,0,1:T(1,128)S(1)}, u32[]{:S(2)}, u32[]{:S(2)}) async-start(f32[1,8,256]{2,0,1:T(1,128)} %compare_select_fusion), calls=%async_computation | async-start | bytes 16384 | tf_op jit(solution)/shard_map/all_to_all | solution.py:158
  18.9 88.5 %all-reduce.4.cloned.1.call-start = ((), (), s32[]{:S(2)}) async-start(), calls=%async_computation.2 | async-start | bytes 294912 | tf_op jit(solution)/shard_map/psum | solution.py:168
  25.0 9.7 %collective-permute-start.9 = (bf16[20,1,16,720]{3,2,0,1:T(8,128)(2,1)S(1)}, bf16[20,1,16,720]{3,2,0,1:T(8,128)(2,1)}, u32[]{:S(2)}, u32[]{:S(2)}) collective-permute-start(bf16[20,1,16,720]{3,2,0,1:T(8,128)(2,1)S(1)} %get-tuple-element.113), channel_id=1, source_target_pairs={{0,4},{4,8},{8,12},{12,16},{16,20},{20,24},{24,28},{28,0},{1,5},{5... | collective-permute-start | bytes 1382408 | tf_op jit(solution)/shard_map/ppermute | solution.py:37
  26.6 3.4 %collective-permute-start.6 = (s32[1,1,256]{2,1,0:T(1,128)S(1)}, s32[1,1,256]{2,1,0:T(1,128)S(1)}, u32[]{:S(2)}, u32[]{:S(2)}) collective-permute-start(s32[1,1,256]{2,1,0:T(1,128)S(1)} %get-tuple-element.124), channel_id=1, source_target_pairs={{0,20},{4,16},{8,28},{12,24},{16,4},{20,0},{24,12},{28,8},{1,21},{... | collective-permute-start | bytes 3080 | tf_op jit(solution)/shard_map/ppermute | solution.py:26
  26.7 7.3 %collective-permute-start.7 = (s32[1,1,256]{2,1,0:T(1,128)S(1)}, s32[1,1,256]{2,1,0:T(1,128)S(1)}, u32[]{:S(2)}, u32[]{:S(2)}) collective-permute-start(s32[1,1,256]{2,1,0:T(1,128)S(1)} %get-tuple-element.130), channel_id=1, source_target_pairs={{0,24},{4,28},{8,16},{12,20},{16,8},{20,12},{24,0},{28,4},{1,25},{... | collective-permute-start | bytes 3080 | tf_op jit(solution)/shard_map/ppermute | solution.py:26
  27.8 6.2 %collective-permute-start.8 = (s32[1,1,256]{2,1,0:T(1,128)S(1)}, s32[1,1,256]{2,1,0:T(1,128)S(1)}, u32[]{:S(2)}, u32[]{:S(2)}) collective-permute-start(s32[1,1,256]{2,1,0:T(1,128)S(1)} %get-tuple-element.123), channel_id=1, source_target_pairs={{0,28},{4,24},{8,20},{12,16},{16,12},{20,8},{24,4},{28,0},{1,29},{... | collective-permute-start | bytes 3080 | tf_op jit(solution)/shard_map/ppermute | solution.py:26
  30.0 93.8 %collective-permute-start = (bf16[20,1,16,720]{3,2,0,1:T(8,128)(2,1)}, bf16[20,1,16,720]{3,2,0,1:T(8,128)(2,1)}, u32[]{:S(2)}, u32[]{:S(2)}) collective-permute-start(bf16[20,1,16,720]{3,2,0,1:T(8,128)(2,1)} %get-tuple-element.115), channel_id=1, source_target_pairs={{0,4},{4,8},{8,12},{12,16},{16,20},{20,24},{24,28},{28,0},{1,5},{5... | collective-permute-start | bytes 1382408 | tf_op jit(solution)/shard_map/ppermute | solution.py:37
  34.0 89.7 %collective-permute-start.1 = (bf16[20,1,16,720]{3,2,0,1:T(8,128)(2,1)S(1)}, bf16[20,1,16,720]{3,2,0,1:T(8,128)(2,1)}, u32[]{:S(2)}, u32[]{:S(2)}) collective-permute-start(bf16[20,1,16,720]{3,2,0,1:T(8,128)(2,1)S(1)} %get-tuple-element.116), channel_id=1, source_target_pairs={{4,0},{8,4},{12,8},{16,12},{20,16},{24,20},{28,24},{0,28},{5,1},{9... | collective-permute-start | bytes 1382408 | tf_op jit(solution)/shard_map/ppermute | solution.py:40
  73.1 8.2 %all-to-all-start.1 = ((f32[1,8,256]{2,0,1:T(1,128)}), f32[1,8,256]{2,0,1:T(1,128)S(1)}, u32[]{:S(2)}, u32[]{:S(2)}) async-start(f32[1,8,256]{2,0,1:T(1,128)} %copy.55), calls=%async_computation.1 | async-start | bytes 16384 | tf_op jit(solution)/shard_map/all_to_all | solution.py:157
  108.4 3.8 %copy-start.2 = (f32[45,720]{1,0:T(8,128)S(1)}, f32[45,720]{1,0:T(8,128)}, u32[]{:S(2)}) copy-start(f32[45,720]{1,0:T(8,128)} %custom-call) | copy-start | bytes 388804
  112.3 11.5 %copy-start.1 = (bf16[20,1,45,720]{3,2,1,0:T(8,128)(2,1)S(1)}, bf16[20,1,45,720]{3,2,1,0:T(8,128)(2,1)}, u32[]{:S(2)}) copy-start(bf16[20,1,45,720]{3,2,1,0:T(8,128)(2,1)} %param.13) | copy-start | bytes 3888004
  115.4 5.1 %collective-permute-start.11 = (f32[1,16,720]{2,1,0:T(8,128)S(1)}, f32[1,16,720]{2,1,0:T(8,128)S(1)}, u32[]{:S(2)}, u32[]{:S(2)}) collective-permute-start(f32[1,16,720]{2,1,0:T(8,128)S(1)} %get-tuple-element.117), channel_id=1, source_target_pairs={{0,4},{4,8},{8,12},{12,16},{16,20},{20,24},{24,28},{28,0},{1,5},{5... | collective-permute-start | bytes 138248 | tf_op jit(solution)/shard_map/ppermute | solution.py:37
  119.3 4.4 %collective-permute-start.12 = (f32[1,16,720]{2,1,0:T(8,128)S(1)}, f32[1,16,720]{2,1,0:T(8,128)S(1)}, u32[]{:S(2)}, u32[]{:S(2)}) collective-permute-start(f32[1,16,720]{2,1,0:T(8,128)S(1)} %get-tuple-element.118), channel_id=1, source_target_pairs={{4,0},{8,4},{12,8},{16,12},{20,16},{24,20},{28,24},{0,28},{5,1},{9... | collective-permute-start | bytes 138248 | tf_op jit(solution)/shard_map/ppermute | solution.py:40
Sparse Core Ops, SparseCore 0:
  73.2 34.1 all-reduce.3
